TPU v7x, 512 devices: a whole 4x4x16 slice. The times are simulated.
512 devices in a mesh: walker: 32 (over z, y_lo), orb: 16 (over x, y_hi, core).
Axes of the slice: x: 4, y: 4 (y_hi: 2, y_lo: 2; y = y_hi * 2 + y_lo), z: 16, core: 2. Of those that a mesh axis runs over, the one named last changes fastest.
Arguments:
- tile_index: int32 [32768], P('walker'), may hold values from 0 to 63
- weights: bfloat16 [32768, 64], P('walker'), may hold values from -0.75 to 0.75
- electron: int32 [32768], P('walker'), may hold values from 0 to 767
- strength: float32 [32768], P('walker'), may hold values from -1.5 to 1.5
- spline_table: bfloat16 [4096, 4096], P(None, 'orb'), may hold values from -6 to 6
- rotation: bfloat16 [4096, 768], P('orb'), may hold values from -0.09375 to 0.09375
- inverse: bfloat16 [32, 768, 768], P('walker', 'orb'), may hold values from -0.21875 to 0.21875
Outputs:
- ratios: float32 [32768], P(('walker', 'orb'))
- gradient: float32 [4096, 768], P('orb')
All inputs are finite; a program needn't handle non-finite values.
Results may differ from a plain program's by a relative error of at most 0.0042.
Values may be sent and summed in bfloat16 or wider, within the bound.
No kernel may reach another device: no remote copies, remote signals or barrier semaphores. Data moves between devices by JAX's collectives and lax.ppermute only.
A program may use at most 64 MiB of HBM per device.

v0:
```python
import jax
import jax.numpy as jnp
from jax import lax
from jax.sharding import PartitionSpec as P


def body(tile_index, weights, electron, strength, spline_table, rotation, inverse):
    points = tile_index.shape[0]
    coeffs = weights.shape[1]
    tiles_count = spline_table.shape[0] // coeffs
    electrons = inverse.shape[2]
    inverse_full = lax.all_gather(inverse[0], "orb", axis=0, tiled=True)
    onehot = (tile_index[:, None] == jnp.arange(tiles_count, dtype=jnp.int32)[None, :]).astype(
        jnp.bfloat16
    )
    stencil_matrix = (onehot[:, :, None] * weights[:, None, :]).reshape(
        points, tiles_count * coeffs
    )
    orbital_values = jnp.dot(
        stencil_matrix, spline_table, preferred_element_type=jnp.float32
    ).astype(jnp.bfloat16)
    pick = (electron[:, None] == jnp.arange(electrons, dtype=jnp.int32)[None, :]).astype(
        jnp.bfloat16
    )
    columns = lax.dot_general(
        pick, inverse_full, (((1,), (1,)), ((), ())), preferred_element_type=jnp.float32
    )
    adjoint = (columns * strength[:, None]).astype(jnp.bfloat16)
    local_gradient = lax.dot_general(
        orbital_values, adjoint, (((0,), (0,)), ((), ())), preferred_element_type=jnp.float32
    )
    rotated_columns = lax.dot_general(
        columns.astype(jnp.bfloat16),
        rotation,
        (((1,), (1,)), ((), ())),
        preferred_element_type=jnp.float32,
    )
    partial_ratio = jnp.sum(orbital_values.astype(jnp.float32) * rotated_columns, axis=1)
    ratios = lax.psum_scatter(partial_ratio, "orb", scatter_dimension=0, tiled=True)
    gradient = lax.psum(local_gradient, "walker")
    return (ratios, gradient)


def solution(mesh):
    in_specs = (
        P("walker"),
        P("walker", None),
        P("walker"),
        P("walker"),
        P(None, "orb"),
        P("orb", None),
        P("walker", "orb", None),
    )
    out_specs = (P(("walker", "orb")), P("orb", None))
    return jax.shard_map(body, mesh=mesh, in_specs=in_specs, out_specs=out_specs, check_vma=False)
```

profile of v0, /device:TPU:4, one launch (start us, length us, event | category | flops | bytes accessed | tf_op | source)
XLA Modules:
  0.0 357.1 jit_solution(11248412728367267794)
XLA Ops:
  7.2 0.0 copy-start
  7.2 0.0 all-gather.3.cloned.1.call-start
  7.2 0.7 all-gather.3.cloned.1.call-update
  7.9 0.0 all-reduce.3.cloned.1.call-start
  8.0 0.7 fusion.13
  8.7 1.5 broadcast_multiply_fusion
  10.1 0.0 copy-done
  10.1 0.0 copy-start.4
  10.2 2.4 convolution_convert_fusion
  12.6 0.0 copy-start.3
  12.6 62.3 %all-gather.3.cloned.1.call-done = bf16[1,768,768]{2,1,0:T(8,128)(2,1)} async-done(((bf16[1,48,768]{2,1,0:T(8,128)(2,1)}), bf16[1,768,768]{2,1,0:T(8,128)(2,1)}) %all-gather.3.cloned.1.call-update) | async-done | bytes 1179664 | tf_op jit(solution)/shard_map/all_gather | solution.py:12
  74.9 0.0 copy-done.4
  74.9 2.8 fusion
  77.7 0.0 copy-start.1
  77.7 1.6 copy-done.1
  79.4 0.0 copy-done.3
  79.4 1.6 fusion.1
  81.0 0.0 all-reduce.3.cloned.1.call-update
  81.0 1.3 dynamic-slice
  82.9 2.5 fusion.9
  85.5 30.2 %all-reduce = f32[1024]{0:T(1024)S(1)} all-reduce(f32[1024]{0:T(1024)S(1)} %fusion.9), channel_id=3, replica_groups=mesh['walker'=32,'orb'=16] {'orb'}, use_global_device_ids=true, to_apply=%region_1.0.clone | all-reduce | flops 1024 | bytes 8192
  115.7 0.6 dynamic-slice.1
  116.3 232.0 %all-reduce.3.cloned.1.call-done = f32[256,768]{1,0:T(8,128)} async-done(((f32[256,768]{1,0:T(8,128)}), f32[256,768]{1,0:T(8,128)}) %all-reduce.3.cloned.1.call-update) | async-done | bytes 786448 | tf_op jit(solution)/shard_map/psum | solution.py:40
  348.2 2.1 copy.11
  (2 shorter events, 0.0 us)
Async XLA Ops:
  7.2 3.0 copy-start
  7.2 67.7 %all-gather.3.cloned.1.call-start = ((), (), s32[]{:S(2)}) async-start(), calls=%async_computation.1 | async-start | bytes 1253376 | tf_op jit(solution)/shard_map/all_gather | solution.py:12
  7.9 340.3 %all-reduce.3.cloned.1.call-start = ((), (), s32[]{:S(2)}) async-start(), calls=%async_computation | async-start | bytes 1572864 | tf_op jit(solution)/shard_map/psum | solution.py:40
  10.1 64.8 %copy-start.4 = (s32[1024]{0:T(1024)S(1)}, s32[1024]{0:T(1024)}, u32[]{:S(2)}) copy-start(s32[1024]{0:T(1024)} %param.9) | copy-start | bytes 12292
  12.6 66.8 %copy-start.3 = (f32[1024]{0:T(1024)S(1)}, f32[1024]{0:T(1024)}, u32[]{:S(2)}) copy-start(f32[1024]{0:T(1024)} %param.10) | copy-start | bytes 12292
  77.7 1.7 copy-start.1
  79.4 3.6 copy-start.2
Sparse Core Ops, SparseCore 0:
  11.3 63.6 all-gather.2
  81.1 267.0 all-reduce.2
where the time goes:
time: 357 us
  waiting for transfers between devices  295 us (83%)
  blocking collectives  30.2 us (8%)
  between operations  14.8 us (4%)
  matrix products  9.31 us (3%)
  local copies, waits for them, and re-layouts  5.59 us (2%)
    psum x1, waiting for transfers between devices, body(): gradient = lax.psum(local_gradient, 'walker')  232 us
    all_gather x1, waiting for transfers between devices, body(): inverse_full = lax.all_gather(inverse[0], 'orb', axis=0, tiled=True)  62.3 us
    unnamed x1, blocking collectives  30.2 us
  transfers between devices with their start and end apart: 2, of which 2 were waited for; matrix products, arithmetic and copies ran while one was open for 3% of the time, Pallas kernels for 0%

commit v1 on v0

--- a/solution.py
+++ b/solution.py
@@ -9,7 +9,13 @@
     coeffs = weights.shape[1]
     tiles_count = spline_table.shape[0] // coeffs
     electrons = inverse.shape[2]
-    inverse_full = lax.all_gather(inverse[0], "orb", axis=0, tiled=True)
+    packet = inverse[0]
+    inverse_full = jnp.concatenate(
+        lax.all_to_all(
+            jnp.stack([packet] * lax.axis_size("orb")), axis_name="orb", split_axis=0, concat_axis=0
+        ),
+        axis=0,
+    )
     onehot = (tile_index[:, None] == jnp.arange(tiles_count, dtype=jnp.int32)[None, :]).astype(
         jnp.bfloat16
     )

time: 357 us -> 319 us (0.89)
  waiting for transfers between devices: 295 us -> 247 us
  starting transfers between devices: 0.08 us -> 10.1 us
    all_gather x1 -> x0, waiting for transfers between devices: 62.3 us -> none  [body(): inverse_full = lax.all_gather(inverse[0], 'orb', axis=0, tiled=True)]
    all_to_all x0 -> x1, waiting for transfers between devices: none -> 14.2 us  [body(): lax.all_to_all(jnp.stack([packet] * lax.axis_size('orb')), axis_name='orb...]
    all_to_all x0 -> x1, starting transfers between devices: none -> 10 us  [body(): lax.all_to_all(jnp.stack([packet] * lax.axis_size('orb')), axis_name='orb...]
  transfers between devices with their start and end apart: 2 -> 2, of which waited for: 2 -> 2; matrix products, arithmetic and copies ran while one was open for 3% -> 2% of each run, Pallas kernels for 0% -> 0%
where the time goes in v1:
time: 319 us; the launch traced here: 318 us
  waiting for transfers between devices  247 us (77%)
  blocking collectives  28.9 us (9%)
  between operations  14.8 us (5%)
  starting transfers between devices  10.1 us (3%)
  matrix products  9.33 us (3%)
  local copies, waits for them, and re-layouts  7.74 us (2%)
    psum x1, waiting for transfers between devices, body(): gradient = lax.psum(local_gradient, 'walker')  233 us
    unnamed x1, blocking collectives  28.9 us
    all_to_all x1, waiting for transfers between devices, body(): lax.all_to_all(jnp.stack([packet] * lax.axis_size('orb')), axis_name='orb...  14.2 us
    all_to_all x1, starting transfers between devices, body(): lax.all_to_all(jnp.stack([packet] * lax.axis_size('orb')), axis_name='orb...  10 us
  transfers between devices with their start and end apart: 2, of which 2 were waited for; matrix products, arithmetic and copies ran while one was open for 2% of the time, Pallas kernels for 0%

profile of v1, /device:TPU:4, one launch (start us, length us, event | category | flops | bytes accessed | tf_op | source)
XLA Modules:
  0.0 318.2 jit_solution(17777520003012769134)
XLA Ops:
  7.2 0.0 copy-start
  7.2 0.0 copy-start.5
  7.2 0.0 copy-start.3
  7.2 2.1 stack.3
  9.3 10.0 %all-to-all-start = ((bf16[16,48,768]{2,1,0:T(8,128)(2,1)}), bf16[16,48,768]{2,1,0:T(8,128)(2,1)}, u32[]{:S(2)}, u32[]{:S(2)}) async-start(bf16[16,48,768]{2,1,0:T(8,128)(2,1)} %stack.3), calls=%async_computation | async-start | bytes 2359296 | tf_op jit(solution)/shard_map/all_to_all | solution.py:14
  19.4 0.0 all-reduce.3.cloned.1.call-start
  19.4 0.0 copy-done.5
  19.5 0.0 copy-done.3
  19.5 0.6 broadcast_multiply_fusion
  20.0 0.0 copy-done
  20.0 0.0 copy-start.6
  20.0 2.4 convolution_convert_fusion
  22.4 14.2 %all-to-all-done = bf16[16,48,768]{2,1,0:T(8,128)(2,1)} async-done(((bf16[16,48,768]{2,1,0:T(8,128)(2,1)}), bf16[16,48,768]{2,1,0:T(8,128)(2,1)}, u32[]{:S(2)}, u32[]{:S(2)}) %all-to-all-start) | async-done | bytes 1179680 | tf_op jit(solution)/shard_map/all_to_all | solution.py:14
  36.6 0.0 copy-done.6
  36.6 2.8 fusion
  39.5 1.6 copy-done.1
  41.1 1.6 fusion.1
  42.7 0.0 all-reduce.3.cloned.1.call-update
  42.8 1.3 dynamic-slice
  44.7 2.5 fusion.9
  47.2 28.9 %all-reduce = f32[1024]{0:T(1024)S(1)} all-reduce(f32[1024]{0:T(1024)S(1)} %fusion.9), channel_id=2, replica_groups=mesh['walker'=32,'orb'=16] {'orb'}, use_global_device_ids=true, to_apply=%region_1.0.clone | all-reduce | flops 1024 | bytes 8192
  76.1 0.6 dynamic-slice.1
  76.7 232.6 %all-reduce.3.cloned.1.call-done = f32[256,768]{1,0:T(8,128)} async-done(((f32[256,768]{1,0:T(8,128)}), f32[256,768]{1,0:T(8,128)}) %all-reduce.3.cloned.1.call-update) | async-done | bytes 786448 | tf_op jit(solution)/shard_map/psum | solution.py:46
  309.3 2.1 copy.11
  (6 shorter events, 0.0 us)
Async XLA Ops:
  7.2 12.9 %copy-start = (bf16[4096,256]{1,0:T(8,128)(2,1)S(1)}, bf16[4096,256]{1,0:T(8,128)(2,1)}, u32[]{:S(2)}) copy-start(bf16[4096,256]{1,0:T(8,128)(2,1)} %param.11) | copy-start | bytes 6291460
  7.2 12.2 %copy-start.5 = (s32[1024]{0:T(1024)S(1)}, s32[1024]{0:T(1024)}, u32[]{:S(2)}) copy-start(s32[1024]{0:T(1024)} %param.7) | copy-start | bytes 12292
  7.2 12.3 %copy-start.3 = (bf16[1024,64]{0,1:T(8,128)(2,1)S(1)}, bf16[1024,64]{0,1:T(8,128)(2,1)}, u32[]{:S(2)}) copy-start(bf16[1024,64]{0,1:T(8,128)(2,1)} %param.8) | copy-start | bytes 393220
  9.3 27.3 %all-to-all-start = ((bf16[16,48,768]{2,1,0:T(8,128)(2,1)}), bf16[16,48,768]{2,1,0:T(8,128)(2,1)}, u32[]{:S(2)}, u32[]{:S(2)}) async-start(bf16[16,48,768]{2,1,0:T(8,128)(2,1)} %stack.3), calls=%async_computation | async-start | bytes 2359296 | tf_op jit(solution)/shard_map/all_to_all | solution.py:14
  19.4 289.9 %all-reduce.3.cloned.1.call-start = ((), (), s32[]{:S(2)}) async-start(), calls=%async_computation.1 | async-start | bytes 1572864 | tf_op jit(solution)/shard_map/psum | solution.py:46
  20.0 16.6 %copy-start.6 = (s32[1024]{0:T(1024)S(1)}, s32[1024]{0:T(1024)}, u32[]{:S(2)}) copy-start(s32[1024]{0:T(1024)} %param.9) | copy-start | bytes 12292
  36.6 4.5 %copy-start.4 = (f32[1024]{0:T(1024)S(1)}, f32[1024]{0:T(1024)}, u32[]{:S(2)}) copy-start(f32[1024]{0:T(1024)} %param.10) | copy-start | bytes 12292
  39.5 1.6 copy-start.1
  41.1 3.6 %copy-start.2 = (bf16[256,768]{1,0:T(8,128)(2,1)S(1)}, bf16[256,768]{1,0:T(8,128)(2,1)}, u32[]{:S(2)}) copy-start(bf16[256,768]{1,0:T(8,128)(2,1)} %param.12) | copy-start | bytes 1179652
Sparse Core Ops, SparseCore 0:
  42.9 266.3 all-reduce.2
